TPU v7x, 256 devices: a whole 4x4x8 slice. The times are simulated.
256 devices in a mesh: seq: 64 (over y, z, core), head: 4 (over x).
Axes of the slice: x: 4, y: 4, z: 8, core: 2. Of those that a mesh axis runs over, the one named last changes fastest.
Arguments:
- queries: bfloat16 [32768, 4096], P(('seq', 'head')), may hold values from -6 to 6
- keys: bfloat16 [32768, 4096], P(('seq', 'head')), may hold values from -6 to 6
- values: bfloat16 [32768, 4096], P(('seq', 'head')), may hold values from -6 to 6
- cluster_ids: int32 [32, 32768, 1], P(None, 'seq'), may hold values from 0 to 127; in each aligned block of 128 rows (0 to 127, 128 to 255, ..., all dimensions but the last counted through in order) at most 2 rows name the same one
- out_weight: bfloat16 [4096, 4096], P('head', 'seq'), may hold values from -0.09375 to 0.09375
Outputs:
- projected: bfloat16 [32768, 4096], P('seq', 'head')
Inputs may be any that keep to these rules, and one draw needn't show every extreme that they name: `cluster_ids`: in each aligned block of 128 tokens of one head (the rows of one device), no cluster id appears more than 2 times, and some cluster appears exactly 2 times.
All inputs are finite; a program needn't handle non-finite values.
Results may differ from a plain program's by a relative error of at most 0.014.
Values may be sent and summed in bfloat16 or wider, within the bound.
No kernel may reach another device: no remote copies, remote signals or barrier semaphores. Data moves between devices by JAX's collectives and lax.ppermute only.
A program may use at most 128 MiB of HBM per device.

v0:
```python
import jax
import jax.numpy as jnp
from jax import lax
from jax.sharding import PartitionSpec as P

HEADS = 32
HD = 128
CLUSTERS = 128


def slot_table(block_ids, slot_depth):
    sub_rows = block_ids.shape[-1]
    onehot = (block_ids[..., None] == jnp.arange(CLUSTERS, dtype=jnp.int32)).astype(jnp.float32)
    lower = (jnp.arange(sub_rows)[:, None] >= jnp.arange(sub_rows)[None, :]).astype(jnp.float32)
    running = jnp.einsum("ts,abse->abte", lower, onehot)
    ranking = (jnp.sum(running * onehot, axis=-1) - 1.0).astype(jnp.int32)
    depth_hit = (ranking[..., None] == jnp.arange(slot_depth, dtype=jnp.int32)).astype(jnp.bfloat16)
    return onehot.astype(jnp.bfloat16)[..., :, None] * depth_hit[..., None, :]


def attend_blocks(packed, validity):
    scores = jnp.einsum(
        "cqd,ckd->cqk", packed[0], packed[1], preferred_element_type=jnp.float32
    ) * HD ** (-0.5)
    scores = jnp.where(validity[:, None, :] > 0, scores, -1e30)
    row_max = jnp.max(scores, axis=-1, keepdims=True)
    raised = jnp.exp(scores - row_max)
    weights = (raised / jnp.sum(raised, axis=-1, keepdims=True)).astype(jnp.bfloat16)
    return jnp.einsum(
        "cqk,ckd->cqd", weights, packed[2], preferred_element_type=jnp.float32
    ).astype(jnp.bfloat16)


def attend_and_return(arrived):
    packed, markers = arrived
    item_count = packed.shape[1]
    n_seq = packed.shape[2]
    lane_count = packed.shape[3]
    result_block = attend_blocks(
        packed.reshape(3, item_count, n_seq * lane_count, HD),
        markers.reshape(item_count, n_seq * lane_count),
    )
    result_block = result_block.reshape(item_count, n_seq, lane_count, HD)
    return lax.all_to_all(result_block, "seq", split_axis=1, concat_axis=1, tiled=True)


def body(queries, keys, values, cluster_ids, out_weight):
    n_seq = lax.axis_size("seq")
    n_head = lax.axis_size("head")
    head_group = lax.axis_index("head")
    tok_dev = cluster_ids.shape[1]
    sub_rows = tok_dev // n_head
    group_heads = HEADS // n_head
    slot_depth = max(2, 2 * tok_dev // (n_head * CLUSTERS))
    lane_count = n_head * slot_depth
    per_owner = group_heads * CLUSTERS // n_seq
    all_ids = cluster_ids[:, :, 0]
    group_ids = lax.dynamic_slice_in_dim(all_ids, head_group * group_heads, group_heads, 0)
    group_ids = group_ids.reshape(group_heads, n_head, sub_rows)
    home_table = slot_table(group_ids, slot_depth)
    relaid = (
        lax.all_to_all(queries, "head", split_axis=1, concat_axis=0, tiled=True),
        lax.all_to_all(keys, "head", split_axis=1, concat_axis=0, tiled=True),
        lax.all_to_all(values, "head", split_axis=1, concat_axis=0, tiled=True),
    )
    stacked = jnp.stack([tensor.reshape(n_head, sub_rows, group_heads, HD) for tensor in relaid])
    packed = jnp.einsum(
        "hltcr,xlthd->xhclrd", home_table, stacked, preferred_element_type=jnp.float32
    ).astype(jnp.bfloat16)
    packed = packed.reshape(3, per_owner, n_seq, lane_count, HD)
    markers = (
        jnp.sum(home_table.astype(jnp.float32), axis=2).transpose(0, 2, 1, 3).astype(jnp.bfloat16)
    )
    markers = markers.reshape(1, per_owner, n_seq, lane_count)
    returned = attend_and_return(
        (
            lax.all_to_all(packed, "seq", split_axis=2, concat_axis=2, tiled=True),
            lax.all_to_all(markers, "seq", split_axis=2, concat_axis=2, tiled=True),
        )
    )
    returned = returned.reshape(group_heads, CLUSTERS, n_head, slot_depth, HD)
    gathered = jnp.einsum(
        "hltcr,hclrd->lthd", home_table, returned, preferred_element_type=jnp.float32
    ).astype(jnp.bfloat16)
    gathered = gathered.reshape(tok_dev, group_heads * HD)
    partial_value = jnp.dot(
        gathered,
        lax.all_gather(out_weight, "seq", axis=1, tiled=True),
        preferred_element_type=jnp.float32,
    )
    return lax.psum_scatter(
        partial_value.astype(jnp.bfloat16), "head", scatter_dimension=1, tiled=True
    )


def solution(mesh):
    in_specs = (
        P(("seq", "head"), None),
        P(("seq", "head"), None),
        P(("seq", "head"), None),
        P(None, "seq", None),
        P("head", "seq"),
    )
    out_specs = P("seq", "head")
    return jax.shard_map(body, mesh=mesh, in_specs=in_specs, out_specs=out_specs, check_vma=False)
```

profile of v0, /device:TPU:1, one launch (start us, length us, event | category | flops | bytes accessed | tf_op | source)
XLA Modules:
  0.0 417.8 jit_solution(13506348038587240276)
XLA Ops:
  6.5 0.0 copy-start
  6.5 0.0 copy-start.2
  6.5 2.4 copy.54
  8.9 4.8 %all-to-all-start.1 = ((bf16[128,4,1024]{0,2,1:T(8,128)(2,1)}), bf16[128,4,1024]{0,2,1:T(8,128)(2,1)S(1)}, u32[]{:S(2)}, u32[]{:S(2)}) async-start(bf16[128,4,1024]{0,2,1:T(8,128)(2,1)} %bitcast.6), calls=%async_computation.1 | async-start | bytes 2097152 | tf_op jit(solution)/shard_map/all_to_all | solution.py:62
  13.7 0.0 copy-done.2
  13.7 1.3 copy.55
  15.1 11.9 %all-to-all-done.1 = bf16[128,4,1024]{0,2,1:T(8,128)(2,1)S(1)} async-done(((bf16[128,4,1024]{0,2,1:T(8,128)(2,1)}), bf16[128,4,1024]{0,2,1:T(8,128)(2,1)S(1)}, u32[]{:S(2)}, u32[]{:S(2)}) %all-to-all-start.1) | async-done | bytes 1048608 | tf_op jit(solution)/shard_map/all_to_all | solution.py:62
  27.0 3.5 all-to-all-start.2
  30.5 2.3 copy.56
  32.8 0.0 copy-done
  32.8 1.2 convert_convert_fusion
  34.0 8.5 %all-to-all-done.2 = bf16[128,4,1024]{0,2,1:T(8,128)(2,1)S(1)} async-done(((bf16[128,4,1024]{0,2,1:T(8,128)(2,1)}), bf16[128,4,1024]{0,2,1:T(8,128)(2,1)S(1)}, u32[]{:S(2)}, u32[]{:S(2)}) %all-to-all-start.2) | async-done | bytes 1048608 | tf_op jit(solution)/shard_map/all_to_all | solution.py:63
  42.5 4.2 %all-to-all-start.3 = ((bf16[128,4,1024]{0,2,1:T(8,128)(2,1)}), bf16[128,4,1024]{0,2,1:T(8,128)(2,1)}, u32[]{:S(2)}, u32[]{:S(2)}) async-start(bf16[128,4,1024]{0,2,1:T(8,128)(2,1)} %bitcast.12), calls=%async_computation.3 | async-start | bytes 2097152 | tf_op jit(solution)/shard_map/all_to_all | solution.py:64
  46.7 0.7 fusion.18
  47.4 1.6 copy.49
  49.1 2.5 multiply_reduce_fusion
  51.6 0.1 reshape.61
  51.7 0.8 copy.52
  52.5 1.3 copy.57
  53.8 0.0 copy-start.3
  53.8 1.3 copy.58
  55.1 2.5 all-to-all-done.3
  57.6 19.1 %all-to-all-start = ((bf16[1,16,64,8]{1,3,0,2:T(8,128)(2,1)}), bf16[1,16,64,8]{1,3,0,2:T(8,128)(2,1)S(1)}, u32[]{:S(2)}, u32[]{:S(2)}) async-start(bf16[1,16,64,8]{1,3,0,2:T(8,128)(2,1)} %copy.52), calls=%async_computation | async-start | bytes 262144 | tf_op jit(solution)/shard_map/all_to_all | solution.py:78
  76.7 1.6 copy.59
  78.3 0.0 copy-done.3
  78.4 3.8 convert_bitcast_fusion
  82.1 2.6 copy.61
  84.8 6.7 %copy.62 = bf16[3,16,64,8,128]{4,1,3,0,2:T(8,128)(2,1)} copy(bf16[3,16,64,8,128]{4,2,1,3,0:T(8,128)(2,1)S(1)} %bitcast.66) | data formatting | bytes 12582912 | tf_op jit(solution)/shard_map/reshape | solution.py:70
  91.4 0.0 all-to-all-done
  91.4 10.5 %all-to-all-start.4 = ((bf16[3,16,64,8,128]{4,1,3,0,2:T(8,128)(2,1)}), bf16[3,16,64,8,128]{4,1,3,0,2:T(8,128)(2,1)}, u32[]{:S(2)}, u32[]{:S(2)}) async-start(bf16[3,16,64,8,128]{4,1,3,0,2:T(8,128)(2,1)} %copy.62), calls=%async_computation.4 | async-start | bytes 12582912 | tf_op jit(solution)/shard_map/all_to_all | solution.py:77
  101.9 0.0 all-gather.2.cloned.1.call-start
  102.0 0.7 all-gather.2.cloned.1.call-update
  102.7 0.3 reduce-scatter.2.cloned.1.call-start
  103.0 0.1 copy.53
  103.1 164.3 %all-to-all-done.4 = bf16[3,16,64,8,128]{4,1,3,0,2:T(8,128)(2,1)} async-done(((bf16[3,16,64,8,128]{4,1,3,0,2:T(8,128)(2,1)}), bf16[3,16,64,8,128]{4,1,3,0,2:T(8,128)(2,1)}, u32[]{:S(2)}, u32[]{:S(2)}) %all-to-all-start.4) | async-done | bytes 6291488 | tf_op jit(solution)/shard_map/all_to_all | solution.py:77
  267.4 6.0 %fusion.45 = (bf16[1,16,64,8,128]{4,1,3,0,2:T(8,128)(2,1)S(1)}, bf16[1,16,64,8,128]{4,1,3,0,2:T(8,128)(2,1)}, bf16[1,16,64,8,128]{4,1,3,0,2:T(8,128)(2,1)S(1)}) fusion(bf16[3,16,64,8,128]{4,1,3,0,2:T(8,128)(2,1)} %all-to-all-done.4), kind=kLoop, calls=%fused_computation.52 | loop fusion | bytes 12582912 | tf_op jit(solution)/shard_map/slice | solution.py:23
  273.4 2.4 fusion.14
  275.8 8.1 %fusion.46 = (f32[16,512]{1,0:T(8,128)S(1)}, f32[16,512,512]{1,2,0:T(8,128)}) fusion(f32[16,512,512]{1,2,0:T(8,128)S(1)} %fusion.14, pred[16,512]{1,0:T(8,128)(4,1)S(1)} %copy.53), kind=kOutput, calls=%fused_computation.53 | output fusion | flops 25166336 | bytes 33595392 | tf_op jit(solution)/shard_map/sub | solution.py:27
  283.9 9.4 %convert_bitcast_fusion.1 = bf16[16,64,8,128]{3,2,1,0:T(8,128)(2,1)S(1)} fusion(bf16[1,16,64,8,128]{4,1,3,0,2:T(8,128)(2,1)} %get-tuple-element.6, f32[16,512,512]{1,2,0:T(8,128)} %get-tuple-element.11, f32[16,512]{1,0:T(8,128)S(1)} %get-tuple-element.10), kind=kOutput, calls=%fused_computation.32 | convolution fusion | flops 1083179008 | bytes 21004288 | tf_op jit(solution)/shard_map/cqk,ckd->cqd/dot_general | solution.py:29
  293.3 2.4 copy.67
  295.8 56.8 %all_to_all.63 = bf16[16,64,8,128]{3,0,2,1:T(8,128)(2,1)S(1)} all-to-all(bf16[16,64,8,128]{3,0,2,1:T(8,128)(2,1)S(1)} %copy.67), channel_id=1, replica_groups=mesh['seq'=64,'head'=4] {'seq'}, dimensions={1} | all-to-all | bytes 4194304 | tf_op jit(solution)/shard_map/all_to_all | solution.py:44
  352.6 1.4 copy.68
  354.0 2.6 fusion.29
  356.5 0.7 copy.70
  357.3 0.0 all-gather.2.cloned.1.call-done
  357.3 0.0 copy-start.1
  357.3 9.5 %convolution_convert_fusion = bf16[512,4096]{1,0:T(8,128)(2,1)} fusion(bf16[1024,4096]{0,1:T(8,128)(2,1)} %all-gather.2.cloned.1.call-done, bf16[64,8,8,128]{3,2,1,0:T(8,128)(2,1)S(1)} %bitcast.70), kind=kOutput, calls=%fused_computation.10 | convolution fusion | flops 4297064448 | bytes 13631488 | tf_op jit(solution)/shard_map/dot_general | solution.py:86
  366.8 0.0 reduce-scatter.2.cloned.1.call-update
  366.8 44.2 %reduce-scatter.2.cloned.1.call-done = bf16[512,1024]{1,0:T(8,128)(2,1)} async-done(((bf16[512,4096]{1,0:T(8,128)(2,1)}), bf16[512,1024]{1,0:T(8,128)(2,1)}) %reduce-scatter.2.cloned.1.call-update) | async-done | bytes 1048592 | tf_op jit(solution)/shard_map/reduce_scatter | solution.py:91
  411.0 0.0 copy-done.1
  (5 shorter events, 0.1 us)
Async XLA Ops:
  6.5 26.2 %copy-start = (s32[32,512,1]{1,2,0:T(1,128)S(1)}, s32[32,512,1]{1,2,0:T(1,128)}, u32[]{:S(2)}) copy-start(s32[32,512,1]{1,2,0:T(1,128)} %param.8) | copy-start | bytes 196612
  6.5 7.2 %copy-start.2 = (bf16[128,4096]{1,0:T(8,128)(2,1)S(1)}, bf16[128,4096]{1,0:T(8,128)(2,1)}, u32[]{:S(2)}) copy-start(bf16[128,4096]{1,0:T(8,128)(2,1)} %param.6) | copy-start | bytes 3145732
  8.9 18.1 %all-to-all-start.1 = ((bf16[128,4,1024]{0,2,1:T(8,128)(2,1)}), bf16[128,4,1024]{0,2,1:T(8,128)(2,1)S(1)}, u32[]{:S(2)}, u32[]{:S(2)}) async-start(bf16[128,4,1024]{0,2,1:T(8,128)(2,1)} %bitcast.6), calls=%async_computation.1 | async-start | bytes 2097152 | tf_op jit(solution)/shard_map/all_to_all | solution.py:62
  27.0 15.5 %all-to-all-start.2 = ((bf16[128,4,1024]{0,2,1:T(8,128)(2,1)}), bf16[128,4,1024]{0,2,1:T(8,128)(2,1)S(1)}, u32[]{:S(2)}, u32[]{:S(2)}) async-start(bf16[128,4,1024]{0,2,1:T(8,128)(2,1)} %bitcast.9), calls=%async_computation.2 | async-start | bytes 2097152 | tf_op jit(solution)/shard_map/all_to_all | solution.py:63
  42.5 15.1 %all-to-all-start.3 = ((bf16[128,4,1024]{0,2,1:T(8,128)(2,1)}), bf16[128,4,1024]{0,2,1:T(8,128)(2,1)}, u32[]{:S(2)}, u32[]{:S(2)}) async-start(bf16[128,4,1024]{0,2,1:T(8,128)(2,1)} %bitcast.12), calls=%async_computation.3 | async-start | bytes 2097152 | tf_op jit(solution)/shard_map/all_to_all | solution.py:64
  53.8 24.6 %copy-start.3 = (bf16[1,4,128,8,128]{4,2,0,1,3:T(8,128)(2,1)S(1)}, bf16[1,4,128,8,128]{4,2,0,1,3:T(8,128)(2,1)}, u32[]{:S(2)}) copy-start(bf16[1,4,128,8,128]{4,2,0,1,3:T(8,128)(2,1)} %copy.57) | copy-start | bytes 3145732
  57.6 33.8 %all-to-all-start = ((bf16[1,16,64,8]{1,3,0,2:T(8,128)(2,1)}), bf16[1,16,64,8]{1,3,0,2:T(8,128)(2,1)S(1)}, u32[]{:S(2)}, u32[]{:S(2)}) async-start(bf16[1,16,64,8]{1,3,0,2:T(8,128)(2,1)} %copy.52), calls=%async_computation | async-start | bytes 262144 | tf_op jit(solution)/shard_map/all_to_all | solution.py:78
  91.4 175.9 %all-to-all-start.4 = ((bf16[3,16,64,8,128]{4,1,3,0,2:T(8,128)(2,1)}), bf16[3,16,64,8,128]{4,1,3,0,2:T(8,128)(2,1)}, u32[]{:S(2)}, u32[]{:S(2)}) async-start(bf16[3,16,64,8,128]{4,1,3,0,2:T(8,128)(2,1)} %copy.62), calls=%async_computation.4 | async-start | bytes 12582912 | tf_op jit(solution)/shard_map/all_to_all | solution.py:77
  101.9 255.3 %all-gather.2.cloned.1.call-start = ((), (), s32[]{:S(2)}) async-start(), calls=%async_computation.7 | async-start | bytes 8519680 | tf_op jit(solution)/shard_map/all_gather | solution.py:88
  102.7 308.3 %reduce-scatter.2.cloned.1.call-start = ((), (), s32[]{:S(2)}) async-start(), calls=%async_computation.8 | async-start | bytes 5242880 | tf_op jit(solution)/shard_map/reduce_scatter | solution.py:91
  357.3 53.7 %copy-start.1 = (s32[32,512,1]{1,2,0:T(1,128)S(1)}, s32[32,512,1]{1,2,0:T(1,128)}, u32[]{:S(2)}) copy-start(s32[32,512,1]{1,2,0:T(1,128)} %param.8) | copy-start | bytes 196612
Sparse Core Ops, SparseCore 0:
  105.6 134.2 all-gather.1
  366.9 43.9 reduce-scatter.1
where the time goes:
time: 418 us
  waiting for transfers between devices  232 us (56%)
  blocking collectives  56.8 us (14%)
  starting transfers between devices  42.5 us (10%)
  local copies, waits for them, and re-layouts  32.7 us (8%)
  matrix products  28.3 us (7%)
  between operations  13.6 us (3%)
  other arithmetic  11.9 us (3%)
    all_to_all x1, waiting for transfers between devices, body(): lax.all_to_all(packed, 'seq', split_axis=2, concat_axis=2, tiled=True)  164 us
    all_to_all x1, blocking collectives, attend_and_return(): lax.all_to_all(result_block, 'seq', split_axis=1, concat_axis=1, tiled=True)  56.8 us
    reduce_scatter x1, waiting for transfers between devices, body(): lax.psum_scatter(partial_value.astype(jnp.bfloat16), 'head', scatter_dime...  44.2 us
    all_to_all x1, starting transfers between devices, body(): lax.all_to_all(markers, 'seq', split_axis=2, concat_axis=2, tiled=True)  19.1 us
    all_to_all x1, waiting for transfers between devices, body(): lax.all_to_all(queries, 'head', split_axis=1, concat_axis=0, tiled=True)  11.9 us
    all_to_all x1, starting transfers between devices, body(): lax.all_to_all(packed, 'seq', split_axis=2, concat_axis=2, tiled=True)  10.5 us
    dot_general x1, matrix products, body(): jnp.dot(gathered, lax.all_gather(out_weight, 'seq', axis=1, tiled=True),...  9.49 us
    dot_general x1, matrix products, attend_blocks(): jnp.einsum('cqk,ckd->cqd', weights, packed[2], preferred_element_type=jnp...  9.4 us
  transfers between devices with their start and end apart: 7, of which 5 were waited for; matrix products, arithmetic and copies ran while one was open for 15% of the time, Pallas kernels for 0%

commit v1 on v0

--- a/solution.py
+++ b/solution.py
@@ -6,6 +6,24 @@
 HEADS = 32
 HD = 128
 CLUSTERS = 128
+
+
+def solve_regions(array_in, where_dim, sheet):
+    o_now = array_in.shape
+    y1 = array_in.reshape(
+        *o_now[:where_dim], sheet, o_now[where_dim] // sheet, *o_now[where_dim + 1 :]
+    )
+    return jnp.moveaxis(y1, where_dim, 0)
+
+
+def _turn_units(vals, array_axis):
+    vals = jnp.moveaxis(vals, 0, array_axis)
+    arr_now = vals.shape
+    return vals.reshape(
+        *arr_now[:array_axis],
+        arr_now[array_axis] * arr_now[array_axis + 1],
+        *arr_now[array_axis + 2 :]
+    )
 
 
 def slot_table(block_ids, slot_depth):
@@ -58,9 +76,26 @@
     group_ids = lax.dynamic_slice_in_dim(all_ids, head_group * group_heads, group_heads, 0)
     group_ids = group_ids.reshape(group_heads, n_head, sub_rows)
     home_table = slot_table(group_ids, slot_depth)
+
+    def ladders_balance(field_in, lane_axis, vec, xin):
+        current_block = jax.lax.psum(1, axis_name=lane_axis)
+        seen_now, spare = (current_block, jax.lax.axis_index(lane_axis))
+        low = solve_regions(field_in, vec, seen_now)
+        trail = [low[spare]]
+        for src_i in range(1, seen_now):
+            arr_out = low[spare ^ src_i]
+            trail.append(
+                jax.lax.ppermute(
+                    arr_out, axis_name=lane_axis, perm=[(ix, ix ^ src_i) for ix in range(seen_now)]
+                )
+            )
+        parts_out = jnp.stack(trail)
+        low = parts_out[spare ^ jnp.arange(seen_now)]
+        return _turn_units(low, xin)
+
     relaid = (
         lax.all_to_all(queries, "head", split_axis=1, concat_axis=0, tiled=True),
-        lax.all_to_all(keys, "head", split_axis=1, concat_axis=0, tiled=True),
+        ladders_balance(keys, "head", 1, 0),
         lax.all_to_all(values, "head", split_axis=1, concat_axis=0, tiled=True),
     )
     stacked = jnp.stack([tensor.reshape(n_head, sub_rows, group_heads, HD) for tensor in relaid])

time: 418 us -> 406 us (0.971)
  waiting for transfers between devices: 232 us -> 220 us
  starting transfers between devices: 42.5 us -> 38.3 us
    all_to_all x1, waiting for transfers between devices: 11.9 us -> 2.16 us  [body(): lax.all_to_all(queries, 'head', split_axis=1, concat_axis=0, tiled=True)]
    all_to_all x1 -> x0, waiting for transfers between devices: 8.49 us -> none  [body(): lax.all_to_all(keys, 'head', split_axis=1, concat_axis=0, tiled=True)]
    all_to_all x1, starting transfers between devices: 19.1 us -> 14.6 us  [body(): lax.all_to_all(markers, 'seq', split_axis=2, concat_axis=2, tiled=True)]
  transfers between devices with their start and end apart: 7 -> 9, of which waited for: 5 -> 5; matrix products, arithmetic and copies ran while one was open for 15% -> 16% of each run, Pallas kernels for 0% -> 0%
where the time goes in v1:
time: 406 us; the launch traced here: 405 us
  waiting for transfers between devices  220 us (54%)
  blocking collectives  56.8 us (14%)
  starting transfers between devices  38.3 us (9%)
  local copies, waits for them, and re-layouts  36.1 us (9%)
  matrix products  28.3 us (7%)
  between operations  13.7 us (3%)
  other arithmetic  12.1 us (3%)
    all_to_all x1, waiting for transfers between devices, body(): lax.all_to_all(packed, 'seq', split_axis=2, concat_axis=2, tiled=True)  164 us
    all_to_all x1, blocking collectives, attend_and_return(): lax.all_to_all(result_block, 'seq', split_axis=1, concat_axis=1, tiled=True)  56.8 us
    reduce_scatter x1, waiting for transfers between devices, body(): lax.psum_scatter(partial_value.astype(jnp.bfloat16), 'head', scatter_dime...  44.1 us
    all_to_all x1, starting transfers between devices, body(): lax.all_to_all(markers, 'seq', split_axis=2, concat_axis=2, tiled=True)  14.6 us
    all_to_all x1, starting transfers between devices, body(): lax.all_to_all(packed, 'seq', split_axis=2, concat_axis=2, tiled=True)  10.5 us
    dot_general x1, matrix products, body(): jnp.dot(gathered, lax.all_gather(out_weight, 'seq', axis=1, tiled=True),...  9.5 us
    dot_general x1, matrix products, attend_blocks(): jnp.einsum('cqk,ckd->cqd', weights, packed[2], preferred_element_type=jnp...  9.4 us
  transfers between devices with their start and end apart: 9, of which 5 were waited for; matrix products, arithmetic and copies ran while one was open for 16% of the time, Pallas kernels for 0%

profile of v1, /device:TPU:1, one launch (start us, length us, event | category | flops | bytes accessed | tf_op | source)
XLA Modules:
  0.0 405.2 jit_solution(6133643032002982691)
XLA Ops:
  6.5 0.0 copy-start
  6.5 0.0 copy-start.4
  6.5 2.3 copy.82
  8.9 4.8 %all-to-all-start.1 = ((bf16[128,4,1024]{0,2,1:T(8,128)(2,1)}), bf16[128,4,1024]{0,2,1:T(8,128)(2,1)S(1)}, u32[]{:S(2)}, u32[]{:S(2)}) async-start(bf16[128,4,1024]{0,2,1:T(8,128)(2,1)} %bitcast.6), calls=%async_computation.1 | async-start | bytes 2097152 | tf_op jit(solution)/shard_map/all_to_all | solution.py:97
  13.7 0.0 copy-done.4
  13.7 0.7 copy.83
  14.4 0.1 constant_dynamic-slice_fusion.3
  14.5 0.8 copy.85
  15.3 1.5 collective-permute-start
  16.8 0.9 copy.86
  17.7 2.4 collective-permute-start.1
  20.0 0.9 copy.87
  20.9 0.0 collective-permute-start.2
  20.9 0.0 copy-done
  20.9 0.3 convert_convert_fusion
  21.2 0.7 copy.77
  21.9 2.3 copy.89
  24.1 0.7 fusion.18
  24.8 2.2 all-to-all-done.1
  27.0 0.0 copy-start.2
  27.0 4.2 %all-to-all-start.2 = ((bf16[128,4,1024]{0,2,1:T(8,128)(2,1)}), bf16[128,4,1024]{0,2,1:T(8,128)(2,1)}, u32[]{:S(2)}, u32[]{:S(2)}) async-start(bf16[128,4,1024]{0,2,1:T(8,128)(2,1)} %bitcast.19), calls=%async_computation.2 | async-start | bytes 2097152 | tf_op jit(solution)/shard_map/all_to_all | solution.py:99
  31.2 2.5 multiply_reduce_fusion
  33.7 0.1 copy.84
  33.9 0.1 reshape.83
  33.9 0.8 copy.80
  34.7 0.0 collective-permute-done
  34.8 3.5 collective-permute-done.1
  38.3 0.0 collective-permute-done.2
  38.3 0.0 copy-done.2
  38.3 1.2 pad_maximum_fusion
  39.6 0.6 gather_fusion
  40.2 0.0 copy-start.3
  40.2 1.3 copy.88
  41.5 1.6 copy.91
  43.1 0.0 copy-done.3
  43.1 1.3 copy.90
  44.5 5.1 %all-to-all-done.2 = bf16[128,4,1024]{0,2,1:T(8,128)(2,1)} async-done(((bf16[128,4,1024]{0,2,1:T(8,128)(2,1)}), bf16[128,4,1024]{0,2,1:T(8,128)(2,1)}, u32[]{:S(2)}, u32[]{:S(2)}) %all-to-all-start.2) | async-done | bytes 1048608 | tf_op jit(solution)/shard_map/all_to_all | solution.py:99
  49.5 14.6 %all-to-all-start = ((bf16[1,16,64,8]{1,3,0,2:T(8,128)(2,1)}), bf16[1,16,64,8]{1,3,0,2:T(8,128)(2,1)S(1)}, u32[]{:S(2)}, u32[]{:S(2)}) async-start(bf16[1,16,64,8]{1,3,0,2:T(8,128)(2,1)} %copy.80), calls=%async_computation | async-start | bytes 262144 | tf_op jit(solution)/shard_map/all_to_all | solution.py:113
  64.1 1.6 copy.92
  65.7 3.8 convert_bitcast_fusion
  69.5 2.6 copy.94
  72.2 6.7 %copy.95 = bf16[3,16,64,8,128]{4,1,3,0,2:T(8,128)(2,1)} copy(bf16[3,16,64,8,128]{4,2,1,3,0:T(8,128)(2,1)S(1)} %bitcast.73) | data formatting | bytes 12582912 | tf_op jit(solution)/shard_map/reshape | solution.py:105
  78.9 0.0 all-to-all-done
  78.9 10.5 %all-to-all-start.3 = ((bf16[3,16,64,8,128]{4,1,3,0,2:T(8,128)(2,1)}), bf16[3,16,64,8,128]{4,1,3,0,2:T(8,128)(2,1)}, u32[]{:S(2)}, u32[]{:S(2)}) async-start(bf16[3,16,64,8,128]{4,1,3,0,2:T(8,128)(2,1)} %copy.95), calls=%async_computation.3 | async-start | bytes 12582912 | tf_op jit(solution)/shard_map/all_to_all | solution.py:112
  89.4 0.0 all-gather.2.cloned.1.call-start
  89.4 0.7 all-gather.2.cloned.1.call-update
  90.1 0.3 reduce-scatter.2.cloned.1.call-start
  90.4 0.1 copy.81
  90.5 164.3 %all-to-all-done.3 = bf16[3,16,64,8,128]{4,1,3,0,2:T(8,128)(2,1)} async-done(((bf16[3,16,64,8,128]{4,1,3,0,2:T(8,128)(2,1)}), bf16[3,16,64,8,128]{4,1,3,0,2:T(8,128)(2,1)}, u32[]{:S(2)}, u32[]{:S(2)}) %all-to-all-start.3) | async-done | bytes 6291488 | tf_op jit(solution)/shard_map/all_to_all | solution.py:112
  254.8 6.0 %fusion.46 = (bf16[1,16,64,8,128]{4,1,3,0,2:T(8,128)(2,1)S(1)}, bf16[1,16,64,8,128]{4,1,3,0,2:T(8,128)(2,1)}, bf16[1,16,64,8,128]{4,1,3,0,2:T(8,128)(2,1)S(1)}) fusion(bf16[3,16,64,8,128]{4,1,3,0,2:T(8,128)(2,1)} %all-to-all-done.3), kind=kLoop, calls=%fused_computation.61 | loop fusion | bytes 12582912 | tf_op jit(solution)/shard_map/slice | solution.py:41
  260.8 2.4 fusion.14
  263.2 8.1 %fusion.47 = (f32[16,512]{1,0:T(8,128)S(1)}, f32[16,512,512]{1,2,0:T(8,128)}) fusion(f32[16,512,512]{1,2,0:T(8,128)S(1)} %fusion.14, pred[16,512]{1,0:T(8,128)(4,1)S(1)} %copy.81), kind=kOutput, calls=%fused_computation.62 | output fusion | flops 25166336 | bytes 33595392 | tf_op jit(solution)/shard_map/sub | solution.py:45
  271.3 9.4 %convert_bitcast_fusion.1 = bf16[16,64,8,128]{3,2,1,0:T(8,128)(2,1)S(1)} fusion(bf16[1,16,64,8,128]{4,1,3,0,2:T(8,128)(2,1)} %get-tuple-element.6, f32[16,512,512]{1,2,0:T(8,128)} %get-tuple-element.15, f32[16,512]{1,0:T(8,128)S(1)} %get-tuple-element.14), kind=kOutput, calls=%fused_computation.33 | convolution fusion | flops 1083179008 | bytes 21004288 | tf_op jit(solution)/shard_map/cqk,ckd->cqd/dot_general | solution.py:47
  280.7 2.4 copy.100
  283.2 56.8 %all_to_all.47 = bf16[16,64,8,128]{3,0,2,1:T(8,128)(2,1)S(1)} all-to-all(bf16[16,64,8,128]{3,0,2,1:T(8,128)(2,1)S(1)} %copy.100), channel_id=1, replica_groups=mesh['seq'=64,'head'=4] {'seq'}, dimensions={1} | all-to-all | bytes 4194304 | tf_op jit(solution)/shard_map/all_to_all | solution.py:62
  340.0 1.4 copy.101
  341.4 2.6 fusion.29
  344.0 0.7 copy.103
  344.7 0.0 all-gather.2.cloned.1.call-done
  344.7 0.0 copy-start.1
  344.7 9.5 %convolution_convert_fusion = bf16[512,4096]{1,0:T(8,128)(2,1)} fusion(bf16[1024,4096]{0,1:T(8,128)(2,1)} %all-gather.2.cloned.1.call-done, bf16[64,8,8,128]{3,2,1,0:T(8,128)(2,1)S(1)} %bitcast.78), kind=kOutput, calls=%fused_computation.11 | convolution fusion | flops 4297064448 | bytes 13631488 | tf_op jit(solution)/shard_map/dot_general | solution.py:121
  354.2 0.0 reduce-scatter.2.cloned.1.call-update
  354.3 44.1 %reduce-scatter.2.cloned.1.call-done = bf16[512,1024]{1,0:T(8,128)(2,1)} async-done(((bf16[512,4096]{1,0:T(8,128)(2,1)}), bf16[512,1024]{1,0:T(8,128)(2,1)}) %reduce-scatter.2.cloned.1.call-update) | async-done | bytes 1048592 | tf_op jit(solution)/shard_map/reduce_scatter | solution.py:126
  398.4 0.0 copy-done.1
  (7 shorter events, 0.1 us)
Async XLA Ops:
  6.5 14.4 %copy-start = (s32[32,512,1]{1,2,0:T(1,128)S(1)}, s32[32,512,1]{1,2,0:T(1,128)}, u32[]{:S(2)}) copy-start(s32[32,512,1]{1,2,0:T(1,128)} %param.8) | copy-start | bytes 196612
  6.5 7.2 %copy-start.4 = (bf16[128,4096]{1,0:T(8,128)(2,1)S(1)}, bf16[128,4096]{1,0:T(8,128)(2,1)}, u32[]{:S(2)}) copy-start(bf16[128,4096]{1,0:T(8,128)(2,1)} %param.6) | copy-start | bytes 3145732
  8.9 18.1 %all-to-all-start.1 = ((bf16[128,4,1024]{0,2,1:T(8,128)(2,1)}), bf16[128,4,1024]{0,2,1:T(8,128)(2,1)S(1)}, u32[]{:S(2)}, u32[]{:S(2)}) async-start(bf16[128,4,1024]{0,2,1:T(8,128)(2,1)} %bitcast.6), calls=%async_computation.1 | async-start | bytes 2097152 | tf_op jit(solution)/shard_map/all_to_all | solution.py:97
  15.3 19.4 %collective-permute-start = (bf16[128,1024]{1,0:T(8,128)(2,1)}, bf16[128,1024]{1,0:T(8,128)(2,1)}, u32[]{:S(2)}, u32[]{:S(2)}) collective-permute-start(bf16[128,1024]{1,0:T(8,128)(2,1)} %bitcast.11), channel_id=1, source_target_pairs={{0,1},{1,0},{2,3},{3,2},{4,5},{5,4},{6,7},{7,6},{8,9},{9,8},{10,11... | collective-permute-start | bytes 786440 | tf_op jit(solution)/shard_map/ppermute | solution.py:88
  17.7 20.6 %collective-permute-start.1 = (bf16[128,1024]{1,0:T(8,128)(2,1)}, bf16[128,1024]{1,0:T(8,128)(2,1)}, u32[]{:S(2)}, u32[]{:S(2)}) collective-permute-start(bf16[128,1024]{1,0:T(8,128)(2,1)} %bitcast.13), channel_id=1, source_target_pairs={{0,2},{1,3},{2,0},{3,1},{4,6},{5,7},{6,4},{7,5},{8,10},{9,11},{10,... | collective-permute-start | bytes 786440 | tf_op jit(solution)/shard_map/ppermute | solution.py:88
  20.9 17.4 %collective-permute-start.2 = (bf16[128,1024]{1,0:T(8,128)(2,1)}, bf16[128,1024]{1,0:T(8,128)(2,1)}, u32[]{:S(2)}, u32[]{:S(2)}) collective-permute-start(bf16[128,1024]{1,0:T(8,128)(2,1)} %bitcast.15), channel_id=1, source_target_pairs={{0,3},{1,2},{2,1},{3,0},{4,7},{5,6},{6,5},{7,4},{8,11},{9,10},{10,... | collective-permute-start | bytes 786440 | tf_op jit(solution)/shard_map/ppermute | solution.py:88
  27.0 11.3 %copy-start.2 = (bf16[128,4,1024]{0,2,1:T(8,128)(2,1)}, bf16[128,4,1024]{0,2,1:T(8,128)(2,1)S(1)}, u32[]{:S(2)}) copy-start(bf16[128,4,1024]{0,2,1:T(8,128)(2,1)S(1)} %all-to-all-done.1) | copy-start | bytes 3145732
  27.0 22.6 %all-to-all-start.2 = ((bf16[128,4,1024]{0,2,1:T(8,128)(2,1)}), bf16[128,4,1024]{0,2,1:T(8,128)(2,1)}, u32[]{:S(2)}, u32[]{:S(2)}) async-start(bf16[128,4,1024]{0,2,1:T(8,128)(2,1)} %bitcast.19), calls=%async_computation.2 | async-start | bytes 2097152 | tf_op jit(solution)/shard_map/all_to_all | solution.py:99
  40.2 3.0 copy-start.3
  49.5 29.3 %all-to-all-start = ((bf16[1,16,64,8]{1,3,0,2:T(8,128)(2,1)}), bf16[1,16,64,8]{1,3,0,2:T(8,128)(2,1)S(1)}, u32[]{:S(2)}, u32[]{:S(2)}) async-start(bf16[1,16,64,8]{1,3,0,2:T(8,128)(2,1)} %copy.80), calls=%async_computation | async-start | bytes 262144 | tf_op jit(solution)/shard_map/all_to_all | solution.py:113
  78.9 175.9 %all-to-all-start.3 = ((bf16[3,16,64,8,128]{4,1,3,0,2:T(8,128)(2,1)}), bf16[3,16,64,8,128]{4,1,3,0,2:T(8,128)(2,1)}, u32[]{:S(2)}, u32[]{:S(2)}) async-start(bf16[3,16,64,8,128]{4,1,3,0,2:T(8,128)(2,1)} %copy.95), calls=%async_computation.3 | async-start | bytes 12582912 | tf_op jit(solution)/shard_map/all_to_all | solution.py:112
  89.4 255.3 %all-gather.2.cloned.1.call-start = ((), (), s32[]{:S(2)}) async-start(), calls=%async_computation.6 | async-start | bytes 8519680 | tf_op jit(solution)/shard_map/all_gather | solution.py:123
  90.1 308.3 %reduce-scatter.2.cloned.1.call-start = ((), (), s32[]{:S(2)}) async-start(), calls=%async_computation.7 | async-start | bytes 5242880 | tf_op jit(solution)/shard_map/reduce_scatter | solution.py:126
  344.7 53.7 %copy-start.1 = (s32[32,512,1]{1,2,0:T(1,128)S(1)}, s32[32,512,1]{1,2,0:T(1,128)}, u32[]{:S(2)}) copy-start(s32[32,512,1]{1,2,0:T(1,128)} %param.8) | copy-start | bytes 196612
Sparse Core Ops, SparseCore 0:
  93.0 134.2 all-gather.1
  354.4 43.9 reduce-scatter.1
